TPU v7x, 512 devices: a whole 4x8x8 slice. The times are simulated.
512 devices in a mesh: grid: 64 (over x, z, core), orb: 8 (over y).
Axes of the slice: x: 4, y: 8, z: 8, core: 2. Of those that a mesh axis runs over, the one named last changes fastest.
Arguments:
- orbitals: float32 [256, 16, 16, 1024], P('grid', None, None, 'orb'), may hold values from -15 to 15
- potential: float32 [256, 16, 16], P('grid'), may hold values from -2 to 0
Outputs:
- filtered: float32 [256, 16, 16, 1024], P('grid', None, None, 'orb')
- hamiltonian_block: float32 [1024, 1024], P('orb', 'grid')
- margin_block: float32 [1024, 1024], P('orb', 'grid')
All inputs are finite; a program needn't handle non-finite values.
Results may differ from a plain program's by a relative error of at most 0.0039.
Values may be sent and summed in bfloat16 or wider, within the bound.
No kernel may reach another device: no remote copies, remote signals or barrier semaphores. Data moves between devices by JAX's collectives and lax.ppermute only.
A program may use at most 64 MiB of HBM per device.

v0:
```python
import jax
import jax.numpy as jnp
from jax import lax
from jax.sharding import PartitionSpec as P

DEGREE = 4
STENCIL = (-205.0 / 72.0, 8.0 / 5.0, -1.0 / 5.0, 8.0 / 315.0, -1.0 / 560.0)
LOWER_EDGE = -2.0
CUT_EDGE = 1.5
UPPER_EDGE = 10.0
EPSILON = 1e-06


def padded_2(shard, sides, width):
    for axis, dim in sides:
        size, length = (lax.axis_size(axis), shard.shape[dim])
        up = [(i, (i + 1) % size) for i in range(size - 1)]
        down = [(j, i) for i, j in up]
        last = lax.slice_in_dim(shard, length - width, length, axis=dim)
        initial = lax.slice_in_dim(shard, 0, width, axis=dim)
        before = lax.ppermute(last, axis, up)
        after = lax.ppermute(initial, axis, down)
        shard = jnp.concatenate([before, shard, after], axis=dim)
    return shard


def plane_matrix(rows_y, cols_x):
    flat_count = rows_y * cols_x
    index_all = jnp.arange(flat_count, dtype=jnp.int32)
    row_y = (index_all // cols_x)[:, None]
    row_x = (index_all % cols_x)[:, None]
    col_y = (index_all // cols_x)[None, :]
    col_x = (index_all % cols_x)[None, :]
    delta_y = jnp.mod(row_y - col_y, rows_y)
    delta_x = jnp.mod(row_x - col_x, cols_x)
    same_y = delta_y == 0
    same_x = delta_x == 0
    matrix = jnp.zeros((flat_count, flat_count), jnp.float32)
    for offset in range(1, 5):
        for signed in (offset, -offset):
            hit_y = jnp.logical_and(same_x, delta_y == signed % rows_y)
            hit_x = jnp.logical_and(same_y, delta_x == signed % cols_x)
            matrix = matrix + STENCIL[offset] * (
                hit_y.astype(jnp.float32) + hit_x.astype(jnp.float32)
            )
    return matrix


def apply_hamiltonian(current, potential, plane):
    layers, rows_y, cols_x, width = current.shape
    padded = padded_2(current.astype(jnp.bfloat16), (("grid", 0),), 4).astype(current.dtype)
    laplacian = 3.0 * STENCIL[0] * current
    for offset in range(1, 5):
        laplacian = laplacian + STENCIL[offset] * (
            padded[4 + offset : 4 + offset + layers] + padded[4 - offset : 4 - offset + layers]
        )
    flat = current.reshape(layers, rows_y * cols_x, width)
    in_plane = jnp.einsum(
        "pq,zqo->zpo",
        plane,
        flat,
        precision=lax.Precision.HIGHEST,
        preferred_element_type=jnp.float32,
    )
    laplacian = laplacian + in_plane.reshape(current.shape)
    return -0.5 * laplacian + potential[:, :, :, None] * current


def chebyshev(initial, potential, plane):
    half_width = (UPPER_EDGE - CUT_EDGE) / 2.0
    centre = (UPPER_EDGE + CUT_EDGE) / 2.0
    sigma_now = half_width / (LOWER_EDGE - centre)
    gamma_ratio = 2.0 / sigma_now
    previous = initial
    current = (
        sigma_now / half_width * (apply_hamiltonian(previous, potential, plane) - centre * previous)
    )
    for degree_step in range(DEGREE - 1):
        sigma_next = 1.0 / (gamma_ratio - sigma_now)
        following = (
            2.0
            * sigma_next
            / half_width
            * (apply_hamiltonian(current, potential, plane) - centre * current)
            - sigma_now * sigma_next * previous
        )
        previous, current, sigma_now = (current, following, sigma_next)
    return current


def contract_points(left_side, right_side):
    return lax.dot_general(
        left_side, right_side, (((0,), (0,)), ((), ())), preferred_element_type=jnp.float32
    )


def on_device(orbitals, potential):
    own_width = orbitals.shape[3]
    point_count = orbitals.shape[0] * orbitals.shape[1] * orbitals.shape[2]
    point_total = float(point_count * lax.axis_size("grid"))
    plane = plane_matrix(orbitals.shape[1], orbitals.shape[2])
    result_block = chebyshev(orbitals, potential, plane)
    own_squares = jnp.sum(result_block * result_block, axis=(0, 1, 2))
    rounded_orbitals = result_block.astype(jnp.bfloat16).reshape(point_count, own_width)
    rounded_image = (
        apply_hamiltonian(result_block, potential, plane)
        .astype(jnp.bfloat16)
        .reshape(point_count, own_width)
    )
    summed_own = lax.psum(own_squares, "grid")
    squares_all = lax.all_gather(summed_own, "orb", axis=0, tiled=True)
    scale_all = 1.0 / jnp.sqrt(squares_all / point_total + EPSILON)
    scale_own = lax.dynamic_slice_in_dim(scale_all, lax.axis_index("orb") * own_width, own_width)
    filtered = result_block * scale_own
    orbitals_all, images_all = (
        lax.all_gather(rounded_orbitals, "orb", axis=1, tiled=True),
        lax.all_gather(rounded_image, "orb", axis=1, tiled=True),
    )
    hamiltonian_part = contract_points(images_all, rounded_orbitals)
    margin_part = contract_points(orbitals_all, rounded_orbitals)
    combined = lax.psum_scatter(
        jnp.concatenate([hamiltonian_part, margin_part], axis=1),
        "grid",
        scatter_dimension=0,
        tiled=True,
    )
    column_count = combined.shape[0]
    column_scale = lax.dynamic_slice_in_dim(
        scale_all, lax.axis_index("grid") * column_count, column_count
    )
    pair_scale = scale_own[:, None] * column_scale[None, :] / point_total
    hamiltonian_block = combined[:, :own_width].T * pair_scale
    margin_block = combined[:, own_width:].T * pair_scale
    return (filtered, hamiltonian_block, margin_block)


def solution(mesh):
    placed = (P("grid", None, None, "orb"), P("grid", None, None))
    return jax.shard_map(
        on_device,
        mesh=mesh,
        in_specs=placed,
        out_specs=(P("grid", None, None, "orb"), P("orb", "grid"), P("orb", "grid")),
        check_vma=False,
    )
```

profile of v0, /device:TPU:8, one launch (start us, length us, event | category | flops | bytes accessed | tf_op | source)
XLA Modules:
  0.0 412.1 jit_solution(13175780743739567016)
XLA Ops:
  7.2 0.0 all-gather.6.cloned.1.call-start
  7.2 1.1 convert_element_type.210
  8.3 1.3 collective-permute-start.1
  9.6 3.0 collective-permute-start
  12.7 0.8 broadcast_multiply_fusion.2
  13.4 2.7 fusion.72
  16.1 0.0 copy-start.1
  16.1 0.0 copy-start.2
  16.1 0.0 collective-permute-done.1
  16.1 0.0 collective-permute-done
  16.1 0.1 maximum_convert_fusion
  16.3 0.9 copy-done.1
  17.1 0.4 fusion.155
  17.5 1.3 collective-permute-start.3
  18.8 4.5 %collective-permute-start.2 = (bf16[4,16,16,128]{3,2,1,0:T(8,128)(2,1)S(1)}, bf16[4,16,16,128]{3,2,1,0:T(8,128)(2,1)S(1)}, u32[]{:S(2)}, u32[]{:S(2)}) collective-permute-start(bf16[4,16,16,128]{3,2,1,0:T(8,128)(2,1)S(1)} %get-tuple-element.18), channel_id=1, source_target_pairs={{0,8},{8,16},{16,24},{24,32},{32,40},{40,48},{48,56},{56,64},{64,7... | collective-permute-start | bytes 786440 | tf_op jit(solution)/shard_map/ppermute | solution.py:21
  23.4 1.9 convolution_bitcast_fusion.3
  25.4 0.2 copy.26
  25.6 0.0 collective-permute-done.2
  25.6 0.1 maximum_convert_fusion.1
  25.7 0.4 fusion.160
  26.2 1.3 collective-permute-start.5
  27.5 5.3 %collective-permute-start.4 = (bf16[4,16,16,128]{3,2,1,0:T(8,128)(2,1)S(1)}, bf16[4,16,16,128]{3,2,1,0:T(8,128)(2,1)S(1)}, u32[]{:S(2)}, u32[]{:S(2)}) collective-permute-start(bf16[4,16,16,128]{3,2,1,0:T(8,128)(2,1)S(1)} %get-tuple-element.16), channel_id=1, source_target_pairs={{0,8},{8,16},{16,24},{24,32},{32,40},{40,48},{48,56},{56,64},{64,7... | collective-permute-start | bytes 786440 | tf_op jit(solution)/shard_map/ppermute | solution.py:21
  32.8 1.9 convolution_bitcast_fusion.2
  34.7 0.2 copy.28
  34.9 0.0 collective-permute-done.5
  35.0 0.0 collective-permute-done.4
  35.0 0.1 maximum_convert_fusion.2
  35.1 0.4 fusion.158
  35.5 1.3 collective-permute-start.7
  36.8 6.2 %collective-permute-start.6 = (bf16[4,16,16,128]{3,2,1,0:T(8,128)(2,1)S(1)}, bf16[4,16,16,128]{3,2,1,0:T(8,128)(2,1)S(1)}, u32[]{:S(2)}, u32[]{:S(2)}) collective-permute-start(bf16[4,16,16,128]{3,2,1,0:T(8,128)(2,1)S(1)} %get-tuple-element.14), channel_id=1, source_target_pairs={{0,8},{8,16},{16,24},{24,32},{32,40},{40,48},{48,56},{56,64},{64,7... | collective-permute-start | bytes 786440 | tf_op jit(solution)/shard_map/ppermute | solution.py:21
  43.0 1.9 convolution_bitcast_fusion.1
  44.9 0.2 copy.30
  45.1 0.0 collective-permute-done.6
  45.1 0.1 maximum_convert_fusion.3
  45.3 1.2 fusion.156
  46.4 0.0 all-gather.6.cloned.1.call-update
  46.4 0.0 all-gather.4.cloned.1.call-start
  46.5 1.3 collective-permute-start.9
  47.8 6.3 %collective-permute-start.8 = (bf16[4,16,16,128]{3,2,1,0:T(8,128)(2,1)}, bf16[4,16,16,128]{3,2,1,0:T(8,128)(2,1)S(1)}, u32[]{:S(2)}, u32[]{:S(2)}) collective-permute-start(bf16[4,16,16,128]{3,2,1,0:T(8,128)(2,1)} %get-tuple-element.12), channel_id=1, source_target_pairs={{0,8},{8,16},{16,24},{24,32},{32,40},{40,48},{48,56},{56,64},{64,7... | collective-permute-start | bytes 786440 | tf_op jit(solution)/shard_map/ppermute | solution.py:21
  54.1 1.9 convolution_bitcast_fusion
  56.1 0.2 multiply_reduce_fusion
  56.2 0.2 copy.32
  56.4 134.8 %psum.7 = f32[128]{0:T(128)S(1)} all-reduce(f32[128]{0:T(128)S(1)} %multiply_reduce_fusion), channel_id=1, replica_groups=mesh['grid'=64,'orb'=8] {'grid'}, use_global_device_ids=true, to_apply=%region_1.2 | all-reduce | flops 128 | bytes 1024 | tf_op jit(solution)/shard_map/psum | solution.py:110
  191.2 15.3 %all-gather = f32[8,1,128]{2,1,0:T(1,128)S(1)} all-gather(f32[1,1,128]{2,1,0:T(1,128)S(1)} %bitcast.65), channel_id=1, replica_groups=mesh['grid'=64,'orb'=8] {'orb'}, dimensions={0}, use_global_device_ids=true | all-gather | bytes 4608 | tf_op jit(solution)/shard_map/all_gather | solution.py:111
  206.5 0.1 dynamic_slice.6
  206.6 0.1 maximum_convert_fusion.4
  206.7 1.3 fusion.5
  208.0 0.0 all-gather.4.cloned.1.call-update
  208.0 0.0 reduce-scatter.4.cloned.1.call-start
  208.1 0.0 all-gather.6.cloned.1.call-done
  208.1 2.1 fusion.165
  210.2 39.9 %all-gather.4.cloned.1.call-done = bf16[1024,1024]{1,0:T(8,128)(2,1)} async-done(((bf16[1024,128]{1,0:T(8,128)(2,1)}), bf16[1024,1024]{1,0:T(8,128)(2,1)}) %all-gather.4.cloned.1.call-update) | async-done | bytes 2097168 | tf_op jit(solution)/shard_map/all_gather | solution.py:117
  250.1 2.1 fusion.164
  252.1 0.1 pad_maximum_fusion
  252.2 1.3 copy.39
  253.6 0.0 reduce-scatter.4.cloned.1.call-update
  253.6 0.1 dynamic_slice.7
  253.7 149.6 %reduce-scatter.4.cloned.1.call-done = f32[16,256]{1,0:T(8,128)} async-done(((f32[1024,256]{1,0:T(8,128)}), f32[16,256]{1,0:T(8,128)}) %reduce-scatter.4.cloned.1.call-update) | async-done | bytes 16400
  403.3 0.7 fusion.163
  404.0 0.1 copy.42
  404.1 0.1 copy.41
  404.2 0.1 bitcast_multiply_fusion
  404.3 0.7 copy.33
  404.9 0.7 copy.34
  (10 shorter events, 0.1 us)
Async XLA Ops:
  7.2 200.9 %all-gather.6.cloned.1.call-start = ((), (), s32[]{:S(2)}) async-start(), calls=%async_computation.2 | async-start | bytes 2359296 | tf_op jit(solution)/shard_map/all_gather | solution.py:116
  8.3 7.8 %collective-permute-start.1 = (bf16[4,16,16,128]{3,2,1,0:T(8,128)(2,1)S(1)}, bf16[4,16,16,128]{3,2,1,0:T(8,128)(2,1)S(1)}, u32[]{:S(2)}, u32[]{:S(2)}) collective-permute-start(bf16[4,16,16,128]{3,2,1,0:T(8,128)(2,1)S(1)} %convert_element_type.210), channel_id=1, source_target_pairs={{8,0},{16,8},{24,16},{32,24},{40,32},{48,40},{56,48},{64,56},{72,6... | collective-permute-start | bytes 786440 | tf_op jit(solution)/shard_map/ppermute | solution.py:22
  9.6 6.5 %collective-permute-start = (bf16[4,16,16,128]{3,2,1,0:T(8,128)(2,1)S(1)}, bf16[4,16,16,128]{3,2,1,0:T(8,128)(2,1)S(1)}, u32[]{:S(2)}, u32[]{:S(2)}) collective-permute-start(bf16[4,16,16,128]{3,2,1,0:T(8,128)(2,1)S(1)} %convert_element_type.210), channel_id=1, source_target_pairs={{0,8},{8,16},{16,24},{24,32},{32,40},{40,48},{48,56},{56,64},{64,7... | collective-permute-start | bytes 786440 | tf_op jit(solution)/shard_map/ppermute | solution.py:21
  16.1 1.0 copy-start.1
  16.1 1.0 copy-start.2
  17.5 8.0 %collective-permute-start.3 = (bf16[4,16,16,128]{3,2,1,0:T(8,128)(2,1)S(1)}, bf16[4,16,16,128]{3,2,1,0:T(8,128)(2,1)S(1)}, u32[]{:S(2)}, u32[]{:S(2)}) collective-permute-start(bf16[4,16,16,128]{3,2,1,0:T(8,128)(2,1)S(1)} %get-tuple-element.18), channel_id=1, source_target_pairs={{8,0},{16,8},{24,16},{32,24},{40,32},{48,40},{56,48},{64,56},{72,6... | collective-permute-start | bytes 786440 | tf_op jit(solution)/shard_map/ppermute | solution.py:22
  18.8 6.7 %collective-permute-start.2 = (bf16[4,16,16,128]{3,2,1,0:T(8,128)(2,1)S(1)}, bf16[4,16,16,128]{3,2,1,0:T(8,128)(2,1)S(1)}, u32[]{:S(2)}, u32[]{:S(2)}) collective-permute-start(bf16[4,16,16,128]{3,2,1,0:T(8,128)(2,1)S(1)} %get-tuple-element.18), channel_id=1, source_target_pairs={{0,8},{8,16},{16,24},{24,32},{32,40},{40,48},{48,56},{56,64},{64,7... | collective-permute-start | bytes 786440 | tf_op jit(solution)/shard_map/ppermute | solution.py:21
  26.2 8.8 %collective-permute-start.5 = (bf16[4,16,16,128]{3,2,1,0:T(8,128)(2,1)S(1)}, bf16[4,16,16,128]{3,2,1,0:T(8,128)(2,1)S(1)}, u32[]{:S(2)}, u32[]{:S(2)}) collective-permute-start(bf16[4,16,16,128]{3,2,1,0:T(8,128)(2,1)S(1)} %get-tuple-element.16), channel_id=1, source_target_pairs={{8,0},{16,8},{24,16},{32,24},{40,32},{48,40},{56,48},{64,56},{72,6... | collective-permute-start | bytes 786440 | tf_op jit(solution)/shard_map/ppermute | solution.py:22
  27.5 7.5 %collective-permute-start.4 = (bf16[4,16,16,128]{3,2,1,0:T(8,128)(2,1)S(1)}, bf16[4,16,16,128]{3,2,1,0:T(8,128)(2,1)S(1)}, u32[]{:S(2)}, u32[]{:S(2)}) collective-permute-start(bf16[4,16,16,128]{3,2,1,0:T(8,128)(2,1)S(1)} %get-tuple-element.16), channel_id=1, source_target_pairs={{0,8},{8,16},{16,24},{24,32},{32,40},{40,48},{48,56},{56,64},{64,7... | collective-permute-start | bytes 786440 | tf_op jit(solution)/shard_map/ppermute | solution.py:21
  35.5 9.6 %collective-permute-start.7 = (bf16[4,16,16,128]{3,2,1,0:T(8,128)(2,1)S(1)}, bf16[4,16,16,128]{3,2,1,0:T(8,128)(2,1)S(1)}, u32[]{:S(2)}, u32[]{:S(2)}) collective-permute-start(bf16[4,16,16,128]{3,2,1,0:T(8,128)(2,1)S(1)} %get-tuple-element.14), channel_id=1, source_target_pairs={{8,0},{16,8},{24,16},{32,24},{40,32},{48,40},{56,48},{64,56},{72,6... | collective-permute-start | bytes 786440 | tf_op jit(solution)/shard_map/ppermute | solution.py:22
  36.8 8.3 %collective-permute-start.6 = (bf16[4,16,16,128]{3,2,1,0:T(8,128)(2,1)S(1)}, bf16[4,16,16,128]{3,2,1,0:T(8,128)(2,1)S(1)}, u32[]{:S(2)}, u32[]{:S(2)}) collective-permute-start(bf16[4,16,16,128]{3,2,1,0:T(8,128)(2,1)S(1)} %get-tuple-element.14), channel_id=1, source_target_pairs={{0,8},{8,16},{16,24},{24,32},{32,40},{40,48},{48,56},{56,64},{64,7... | collective-permute-start | bytes 786440 | tf_op jit(solution)/shard_map/ppermute | solution.py:21
  46.4 203.6 %all-gather.4.cloned.1.call-start = ((), (), s32[]{:S(2)}) async-start(), calls=%async_computation.1 | async-start | bytes 2359296 | tf_op jit(solution)/shard_map/all_gather | solution.py:117
  46.5 160.1 %collective-permute-start.9 = (bf16[4,16,16,128]{3,2,1,0:T(8,128)(2,1)}, bf16[4,16,16,128]{3,2,1,0:T(8,128)(2,1)S(1)}, u32[]{:S(2)}, u32[]{:S(2)}) collective-permute-start(bf16[4,16,16,128]{3,2,1,0:T(8,128)(2,1)} %get-tuple-element.12), channel_id=1, source_target_pairs={{8,0},{16,8},{24,16},{32,24},{40,32},{48,40},{56,48},{64,56},{72,6... | collective-permute-start | bytes 786440 | tf_op jit(solution)/shard_map/ppermute | solution.py:22
  47.8 158.8 %collective-permute-start.8 = (bf16[4,16,16,128]{3,2,1,0:T(8,128)(2,1)}, bf16[4,16,16,128]{3,2,1,0:T(8,128)(2,1)S(1)}, u32[]{:S(2)}, u32[]{:S(2)}) collective-permute-start(bf16[4,16,16,128]{3,2,1,0:T(8,128)(2,1)} %get-tuple-element.12), channel_id=1, source_target_pairs={{0,8},{8,16},{16,24},{24,32},{32,40},{40,48},{48,56},{56,64},{64,7... | collective-permute-start | bytes 786440 | tf_op jit(solution)/shard_map/ppermute | solution.py:21
  56.1 150.5 %copy-start = (bf16[4,16,16,128]{3,2,1,0:T(8,128)(2,1)S(1)}, bf16[4,16,16,128]{3,2,1,0:T(8,128)(2,1)}, u32[]{:S(2)}) copy-start(bf16[4,16,16,128]{3,2,1,0:T(8,128)(2,1)} %get-tuple-element.12) | copy-start | bytes 786436
  208.0 195.2 %reduce-scatter.4.cloned.1.call-start = ((), (), s32[]{:S(2)}) async-start(), calls=%async_computation.3 | async-start | bytes 1064960
Sparse Core Ops, SparseCore 0:
  46.6 66.5 all-gather.5
  208.2 41.8 all-gather.3
  254.6 148.5 reduce-scatter.3
where the time goes:
time: 413 us; the launch traced here: 412 us
  waiting for transfers between devices  190 us (46%)
  blocking collectives  150 us (36%)
  starting transfers between devices  32 us (8%)
  matrix products  14.5 us (4%)
  between operations  14.1 us (3%)
  other arithmetic  6.55 us (2%)
  local copies, waits for them, and re-layouts  5.38 us (1%)
    unnamed x4, waiting for transfers between devices  150 us
    psum x1, blocking collectives, on_device(): summed_own = lax.psum(own_squares, 'grid')  135 us
    all_gather x1, waiting for transfers between devices, on_device(): lax.all_gather(rounded_image, 'orb', axis=1, tiled=True)  39.9 us
    ppermute x5, starting transfers between devices, padded_2(): before = lax.ppermute(last, axis, up)  25.4 us
    all_gather x1, blocking collectives, on_device(): squares_all = lax.all_gather(summed_own, 'orb', axis=0, tiled=True)  15.3 us
    dot_general x5, matrix products, apply_hamiltonian(): jnp.einsum('pq,zqo->zpo', plane, flat, precision=lax.Precision.HIGHEST, p...  10.4 us
  transfers between devices with their start and end apart: 13, of which 2 were waited for; matrix products, arithmetic and copies ran while one was open for 4% of the time, Pallas kernels for 0%

commit v1 on v0

--- a/solution.py
+++ b/solution.py
@@ -9,6 +9,12 @@
 CUT_EDGE = 1.5
 UPPER_EDGE = 10.0
 EPSILON = 1e-06
+
+
+def laid_out(parts, dim):
+    parts = jnp.moveaxis(parts, 0, dim)
+    shape = parts.shape
+    return parts.reshape(*shape[:dim], shape[dim] * shape[dim + 1], *shape[dim + 2 :])
 
 
 def padded_2(shard, sides, width):
@@ -108,7 +114,19 @@
         .reshape(point_count, own_width)
     )
     summed_own = lax.psum(own_squares, "grid")
-    squares_all = lax.all_gather(summed_own, "orb", axis=0, tiled=True)
+    count = lax.axis_size("orb")
+    pairs = [(i_2, (i_2 + 1) % count) for i_2 in range(count)]
+    back = [(b, a) for a, b in pairs]
+    lower, upper = ([], [])
+    for step in range(count - 1):
+        if step % 2 == 0:
+            lower.append(lax.ppermute(lower[-1] if lower else summed_own, "orb", pairs))
+        else:
+            upper.append(lax.ppermute(upper[-1] if upper else summed_own, "orb", back))
+    parts = jnp.stack([*lower[::-1], summed_own, *upper])
+    shift = lax.axis_index("orb") - len(lower)
+    parts = parts[(jnp.arange(count) - shift) % count]
+    squares_all = laid_out(parts, 0)
     scale_all = 1.0 / jnp.sqrt(squares_all / point_total + EPSILON)
     scale_own = lax.dynamic_slice_in_dim(scale_all, lax.axis_index("orb") * own_width, own_width)
     filtered = result_block * scale_own

time: 413 us -> 422 us (1.022)
  starting transfers between devices: 32 us -> 51.4 us
  blocking collectives: 150 us -> 135 us
    ppermute x0 -> x7, starting transfers between devices: none -> 22.7 us  [the longest x4 14.7 us: on_device(): lower.append(lax.ppermute(lower[-1] if lower else summed_own, 'orb', pairs))]
    all_gather x1 -> x0, blocking collectives: 15.3 us -> none  [on_device(): squares_all = lax.all_gather(summed_own, 'orb', axis=0, tiled=True)]
  transfers between devices with their start and end apart: 13 -> 20, of which waited for: 2 -> 3; matrix products, arithmetic and copies ran while one was open for 4% -> 4% of each run, Pallas kernels for 0% -> 0%
where the time goes in v1:
time: 422 us; the launch traced here: 421 us
  waiting for transfers between devices  194 us (46%)
  blocking collectives  135 us (32%)
  starting transfers between devices  51.4 us (12%)
  matrix products  14.5 us (3%)
  between operations  14.2 us (3%)
  other arithmetic  6.55 us (2%)
  local copies, waits for them, and re-layouts  5.99 us (1%)
    unnamed x4, waiting for transfers between devices  150 us
    psum x1, blocking collectives, on_device(): summed_own = lax.psum(own_squares, 'grid')  135 us
    all_gather x1, waiting for transfers between devices, on_device(): lax.all_gather(rounded_image, 'orb', axis=1, tiled=True)  43.7 us
    ppermute x5, starting transfers between devices, padded_2(): before = lax.ppermute(last, axis, up)  22.1 us
    ppermute x4, starting transfers between devices, on_device(): lower.append(lax.ppermute(lower[-1] if lower else summed_own, 'orb', pairs))  14.7 us
    dot_general x5, matrix products, apply_hamiltonian(): jnp.einsum('pq,zqo->zpo', plane, flat, precision=lax.Precision.HIGHEST, p...  10.4 us
  transfers between devices with their start and end apart: 20, of which 3 were waited for; matrix products, arithmetic and copies ran while one was open for 4% of the time, Pallas kernels for 0%

profile of v1, /device:TPU:8, one launch (start us, length us, event | category | flops | bytes accessed | tf_op | source)
XLA Modules:
  0.0 421.5 jit_solution(4004824662247317748)
XLA Ops:
  7.2 0.0 all-gather.5.cloned.1.call-start
  7.2 1.1 convert_element_type.210
  8.3 1.3 collective-permute-start.1
  9.6 3.0 collective-permute-start
  12.7 0.8 broadcast_multiply_fusion.2
  13.4 2.7 fusion.72
  16.1 0.1 maximum_convert_fusion
  16.3 0.9 copy-done.1
  17.1 0.4 fusion.157
  17.5 1.3 collective-permute-start.3
  18.8 4.5 %collective-permute-start.2 = (bf16[4,16,16,128]{3,2,1,0:T(8,128)(2,1)S(1)}, bf16[4,16,16,128]{3,2,1,0:T(8,128)(2,1)S(1)}, u32[]{:S(2)}, u32[]{:S(2)}) collective-permute-start(bf16[4,16,16,128]{3,2,1,0:T(8,128)(2,1)S(1)} %get-tuple-element.18), channel_id=1, source_target_pairs={{0,8},{8,16},{16,24},{24,32},{32,40},{40,48},{48,56},{56,64},{64,7... | collective-permute-start | bytes 786440 | tf_op jit(solution)/shard_map/ppermute | solution.py:27
  23.4 1.9 convolution_bitcast_fusion.3
  25.4 0.2 copy.26
  25.6 0.1 maximum_convert_fusion.1
  25.7 0.4 fusion.162
  26.2 1.3 collective-permute-start.5
  27.5 5.3 %collective-permute-start.4 = (bf16[4,16,16,128]{3,2,1,0:T(8,128)(2,1)S(1)}, bf16[4,16,16,128]{3,2,1,0:T(8,128)(2,1)S(1)}, u32[]{:S(2)}, u32[]{:S(2)}) collective-permute-start(bf16[4,16,16,128]{3,2,1,0:T(8,128)(2,1)S(1)} %get-tuple-element.16), channel_id=1, source_target_pairs={{0,8},{8,16},{16,24},{24,32},{32,40},{40,48},{48,56},{56,64},{64,7... | collective-permute-start | bytes 786440 | tf_op jit(solution)/shard_map/ppermute | solution.py:27
  32.8 1.9 convolution_bitcast_fusion.2
  34.7 0.2 copy.28
  35.0 0.1 maximum_convert_fusion.2
  35.1 0.4 fusion.160
  35.5 1.3 collective-permute-start.7
  36.8 6.2 %collective-permute-start.6 = (bf16[4,16,16,128]{3,2,1,0:T(8,128)(2,1)S(1)}, bf16[4,16,16,128]{3,2,1,0:T(8,128)(2,1)S(1)}, u32[]{:S(2)}, u32[]{:S(2)}) collective-permute-start(bf16[4,16,16,128]{3,2,1,0:T(8,128)(2,1)S(1)} %get-tuple-element.14), channel_id=1, source_target_pairs={{0,8},{8,16},{16,24},{24,32},{32,40},{40,48},{48,56},{56,64},{64,7... | collective-permute-start | bytes 786440 | tf_op jit(solution)/shard_map/ppermute | solution.py:27
  43.0 1.9 convolution_bitcast_fusion.1
  44.9 0.2 copy.30
  45.1 0.1 maximum_convert_fusion.3
  45.3 1.1 fusion.158
  46.4 0.0 all-gather.5.cloned.1.call-update
  46.4 0.0 all-gather.3.cloned.1.call-start
  46.5 0.2 multiply_reduce_fusion
  46.6 134.7 %psum.7 = f32[128]{0:T(128)S(1)} all-reduce(f32[128]{0:T(128)S(1)} %multiply_reduce_fusion), channel_id=1, replica_groups=mesh['grid'=64,'orb'=8] {'grid'}, use_global_device_ids=true, to_apply=%region_1.2 | all-reduce | flops 128 | bytes 1024 | tf_op jit(solution)/shard_map/psum | solution.py:116
  181.4 3.5 collective-permute-start.8
  184.9 2.4 collective-permute-start.12
  187.3 3.5 collective-permute-start.9
  190.8 2.4 collective-permute-start.13
  193.2 3.8 collective-permute-start.10
  197.0 1.3 collective-permute-start.16
  198.3 3.0 collective-permute-start.15
  201.4 3.3 collective-permute-start.14
  204.7 3.9 collective-permute-start.11
  208.6 1.9 convolution_bitcast_fusion
  210.6 0.2 copy.32
  210.8 0.6 collective-permute-done.11
  211.4 0.6 gather_fusion
  211.9 0.1 dynamic_slice.6
  212.0 0.1 maximum_convert_fusion.4
  212.2 1.3 fusion.5
  213.4 0.0 all-gather.3.cloned.1.call-update
  213.5 0.0 reduce-scatter.4.cloned.1.call-start
  213.5 0.0 all-gather.5.cloned.1.call-done
  213.5 2.1 fusion.167
  215.6 43.7 %all-gather.3.cloned.1.call-done = bf16[1024,1024]{1,0:T(8,128)(2,1)} async-done(((bf16[1024,128]{1,0:T(8,128)(2,1)}), bf16[1024,1024]{1,0:T(8,128)(2,1)}) %all-gather.3.cloned.1.call-update) | async-done | bytes 2097168 | tf_op jit(solution)/shard_map/all_gather | solution.py:135
  259.4 2.1 fusion.166
  261.4 0.1 pad_maximum_fusion
  261.6 1.4 copy.39
  262.9 0.0 reduce-scatter.4.cloned.1.call-update
  262.9 0.1 dynamic_slice.7
  263.0 149.6 %reduce-scatter.4.cloned.1.call-done = f32[16,256]{1,0:T(8,128)} async-done(((f32[1024,256]{1,0:T(8,128)}), f32[16,256]{1,0:T(8,128)}) %reduce-scatter.4.cloned.1.call-update) | async-done | bytes 16400
  412.6 0.7 fusion.165
  413.3 0.1 copy.42
  413.4 0.1 copy.41
  413.5 0.1 bitcast_multiply_fusion
  413.6 0.7 copy.33
  414.3 0.7 copy.34
  (27 shorter events, 0.2 us)
Async XLA Ops:
  7.2 206.4 %all-gather.5.cloned.1.call-start = ((), (), s32[]{:S(2)}) async-start(), calls=%async_computation.2 | async-start | bytes 2359296 | tf_op jit(solution)/shard_map/all_gather | solution.py:134
  8.3 7.8 %collective-permute-start.1 = (bf16[4,16,16,128]{3,2,1,0:T(8,128)(2,1)S(1)}, bf16[4,16,16,128]{3,2,1,0:T(8,128)(2,1)S(1)}, u32[]{:S(2)}, u32[]{:S(2)}) collective-permute-start(bf16[4,16,16,128]{3,2,1,0:T(8,128)(2,1)S(1)} %convert_element_type.210), channel_id=1, source_target_pairs={{8,0},{16,8},{24,16},{32,24},{40,32},{48,40},{56,48},{64,56},{72,6... | collective-permute-start | bytes 786440 | tf_op jit(solution)/shard_map/ppermute | solution.py:28
  9.6 6.5 %collective-permute-start = (bf16[4,16,16,128]{3,2,1,0:T(8,128)(2,1)S(1)}, bf16[4,16,16,128]{3,2,1,0:T(8,128)(2,1)S(1)}, u32[]{:S(2)}, u32[]{:S(2)}) collective-permute-start(bf16[4,16,16,128]{3,2,1,0:T(8,128)(2,1)S(1)} %convert_element_type.210), channel_id=1, source_target_pairs={{0,8},{8,16},{16,24},{24,32},{32,40},{40,48},{48,56},{56,64},{64,7... | collective-permute-start | bytes 786440 | tf_op jit(solution)/shard_map/ppermute | solution.py:27
  16.1 1.0 copy-start.1
  16.1 1.0 copy-start.2
  17.5 8.0 %collective-permute-start.3 = (bf16[4,16,16,128]{3,2,1,0:T(8,128)(2,1)S(1)}, bf16[4,16,16,128]{3,2,1,0:T(8,128)(2,1)S(1)}, u32[]{:S(2)}, u32[]{:S(2)}) collective-permute-start(bf16[4,16,16,128]{3,2,1,0:T(8,128)(2,1)S(1)} %get-tuple-element.18), channel_id=1, source_target_pairs={{8,0},{16,8},{24,16},{32,24},{40,32},{48,40},{56,48},{64,56},{72,6... | collective-permute-start | bytes 786440 | tf_op jit(solution)/shard_map/ppermute | solution.py:28
  18.8 6.7 %collective-permute-start.2 = (bf16[4,16,16,128]{3,2,1,0:T(8,128)(2,1)S(1)}, bf16[4,16,16,128]{3,2,1,0:T(8,128)(2,1)S(1)}, u32[]{:S(2)}, u32[]{:S(2)}) collective-permute-start(bf16[4,16,16,128]{3,2,1,0:T(8,128)(2,1)S(1)} %get-tuple-element.18), channel_id=1, source_target_pairs={{0,8},{8,16},{16,24},{24,32},{32,40},{40,48},{48,56},{56,64},{64,7... | collective-permute-start | bytes 786440 | tf_op jit(solution)/shard_map/ppermute | solution.py:27
  26.2 8.8 %collective-permute-start.5 = (bf16[4,16,16,128]{3,2,1,0:T(8,128)(2,1)S(1)}, bf16[4,16,16,128]{3,2,1,0:T(8,128)(2,1)S(1)}, u32[]{:S(2)}, u32[]{:S(2)}) collective-permute-start(bf16[4,16,16,128]{3,2,1,0:T(8,128)(2,1)S(1)} %get-tuple-element.16), channel_id=1, source_target_pairs={{8,0},{16,8},{24,16},{32,24},{40,32},{48,40},{56,48},{64,56},{72,6... | collective-permute-start | bytes 786440 | tf_op jit(solution)/shard_map/ppermute | solution.py:28
  27.5 7.5 %collective-permute-start.4 = (bf16[4,16,16,128]{3,2,1,0:T(8,128)(2,1)S(1)}, bf16[4,16,16,128]{3,2,1,0:T(8,128)(2,1)S(1)}, u32[]{:S(2)}, u32[]{:S(2)}) collective-permute-start(bf16[4,16,16,128]{3,2,1,0:T(8,128)(2,1)S(1)} %get-tuple-element.16), channel_id=1, source_target_pairs={{0,8},{8,16},{16,24},{24,32},{32,40},{40,48},{48,56},{56,64},{64,7... | collective-permute-start | bytes 786440 | tf_op jit(solution)/shard_map/ppermute | solution.py:27
  35.5 9.6 %collective-permute-start.7 = (bf16[4,16,16,128]{3,2,1,0:T(8,128)(2,1)S(1)}, bf16[4,16,16,128]{3,2,1,0:T(8,128)(2,1)S(1)}, u32[]{:S(2)}, u32[]{:S(2)}) collective-permute-start(bf16[4,16,16,128]{3,2,1,0:T(8,128)(2,1)S(1)} %get-tuple-element.14), channel_id=1, source_target_pairs={{8,0},{16,8},{24,16},{32,24},{40,32},{48,40},{56,48},{64,56},{72,6... | collective-permute-start | bytes 786440 | tf_op jit(solution)/shard_map/ppermute | solution.py:28
  36.8 8.3 %collective-permute-start.6 = (bf16[4,16,16,128]{3,2,1,0:T(8,128)(2,1)S(1)}, bf16[4,16,16,128]{3,2,1,0:T(8,128)(2,1)S(1)}, u32[]{:S(2)}, u32[]{:S(2)}) collective-permute-start(bf16[4,16,16,128]{3,2,1,0:T(8,128)(2,1)S(1)} %get-tuple-element.14), channel_id=1, source_target_pairs={{0,8},{8,16},{16,24},{24,32},{32,40},{40,48},{48,56},{56,64},{64,7... | collective-permute-start | bytes 786440 | tf_op jit(solution)/shard_map/ppermute | solution.py:27
  46.4 212.9 %all-gather.3.cloned.1.call-start = ((), (), s32[]{:S(2)}) async-start(), calls=%async_computation.1 | async-start | bytes 2359296 | tf_op jit(solution)/shard_map/all_gather | solution.py:135
  181.4 5.9 %collective-permute-start.8 = (f32[128]{0:T(128)S(1)}, f32[128]{0:T(128)S(1)}, u32[]{:S(2)}, u32[]{:S(2)}) collective-permute-start(f32[128]{0:T(128)S(1)} %psum.7), channel_id=1, source_target_pairs={{0,1},{1,2},{2,3},{3,4},{4,5},{5,6},{6,7},{7,0},{8,9},{9,10},{10,1... | collective-permute-start | bytes 1544 | tf_op jit(solution)/shard_map/ppermute | solution.py:123
  184.9 5.9 %collective-permute-start.12 = (f32[128]{0:T(128)S(1)}, f32[128]{0:T(128)S(1)}, u32[]{:S(2)}, u32[]{:S(2)}) collective-permute-start(f32[128]{0:T(128)S(1)} %psum.7), channel_id=1, source_target_pairs={{1,0},{2,1},{3,2},{4,3},{5,4},{6,5},{7,6},{0,7},{9,8},{10,9},{11,1... | collective-permute-start | bytes 1544 | tf_op jit(solution)/shard_map/ppermute | solution.py:125
  187.3 5.9 %collective-permute-start.9 = (f32[128]{0:T(128)S(1)}, f32[128]{0:T(128)S(1)}, u32[]{:S(2)}, u32[]{:S(2)}) collective-permute-start(f32[128]{0:T(128)S(1)} %collective-permute-done.8), channel_id=1, source_target_pairs={{0,1},{1,2},{2,3},{3,4},{4,5},{5,6},{6,7},{7,0},{8,9},{9,10},{10,1... | collective-permute-start | bytes 1544 | tf_op jit(solution)/shard_map/ppermute | solution.py:123
  190.8 10.6 %collective-permute-start.13 = (f32[128]{0:T(128)S(1)}, f32[128]{0:T(128)S(1)}, u32[]{:S(2)}, u32[]{:S(2)}) collective-permute-start(f32[128]{0:T(128)S(1)} %collective-permute-done.12), channel_id=1, source_target_pairs={{1,0},{2,1},{3,2},{4,3},{5,4},{6,5},{7,6},{0,7},{9,8},{10,9},{11,1... | collective-permute-start | bytes 1544 | tf_op jit(solution)/shard_map/ppermute | solution.py:125
  193.2 11.5 %collective-permute-start.10 = (f32[128]{0:T(128)S(1)}, f32[128]{0:T(128)S(1)}, u32[]{:S(2)}, u32[]{:S(2)}) collective-permute-start(f32[128]{0:T(128)S(1)} %collective-permute-done.9), channel_id=1, source_target_pairs={{0,1},{1,2},{2,3},{3,4},{4,5},{5,6},{6,7},{7,0},{8,9},{9,10},{10,1... | collective-permute-start | bytes 1544 | tf_op jit(solution)/shard_map/ppermute | solution.py:123
  197.0 15.0 %collective-permute-start.16 = (bf16[4,16,16,128]{3,2,1,0:T(8,128)(2,1)}, bf16[4,16,16,128]{3,2,1,0:T(8,128)(2,1)S(1)}, u32[]{:S(2)}, u32[]{:S(2)}) collective-permute-start(bf16[4,16,16,128]{3,2,1,0:T(8,128)(2,1)} %get-tuple-element.12), channel_id=1, source_target_pairs={{8,0},{16,8},{24,16},{32,24},{40,32},{48,40},{56,48},{64,56},{72,6... | collective-permute-start | bytes 786440 | tf_op jit(solution)/shard_map/ppermute | solution.py:28
  198.3 13.7 %collective-permute-start.15 = (bf16[4,16,16,128]{3,2,1,0:T(8,128)(2,1)}, bf16[4,16,16,128]{3,2,1,0:T(8,128)(2,1)S(1)}, u32[]{:S(2)}, u32[]{:S(2)}) collective-permute-start(bf16[4,16,16,128]{3,2,1,0:T(8,128)(2,1)} %get-tuple-element.12), channel_id=1, source_target_pairs={{0,8},{8,16},{16,24},{24,32},{32,40},{40,48},{48,56},{56,64},{64,7... | collective-permute-start | bytes 786440 | tf_op jit(solution)/shard_map/ppermute | solution.py:27
  201.4 9.4 %collective-permute-start.14 = (f32[128]{0:T(128)S(1)}, f32[128]{0:T(128)S(1)}, u32[]{:S(2)}, u32[]{:S(2)}) collective-permute-start(f32[128]{0:T(128)S(1)} %collective-permute-done.13), channel_id=1, source_target_pairs={{1,0},{2,1},{3,2},{4,3},{5,4},{6,5},{7,6},{0,7},{9,8},{10,9},{11,1... | collective-permute-start | bytes 1544 | tf_op jit(solution)/shard_map/ppermute | solution.py:125
  204.7 6.7 %collective-permute-start.11 = (f32[128]{0:T(128)S(1)}, f32[128]{0:T(128)S(1)}, u32[]{:S(2)}, u32[]{:S(2)}) collective-permute-start(f32[128]{0:T(128)S(1)} %collective-permute-done.10), channel_id=1, source_target_pairs={{0,1},{1,2},{2,3},{3,4},{4,5},{5,6},{6,7},{7,0},{8,9},{9,10},{10,1... | collective-permute-start | bytes 1544 | tf_op jit(solution)/shard_map/ppermute | solution.py:123
  208.6 3.4 copy-start
  213.5 199.1 %reduce-scatter.4.cloned.1.call-start = ((), (), s32[]{:S(2)}) async-start(), calls=%async_computation.3 | async-start | bytes 1064960
Sparse Core Ops, SparseCore 0:
  46.6 66.4 all-gather.4
  213.6 45.7 all-gather.2
  263.9 148.5 reduce-scatter.3
